TPU v7x, 32 devices: a whole 2x2x4 slice. The times are simulated.
32 devices in a mesh: groups: 2 (over y), ctx: 4 (over z), head: 4 (over x, core).
Axes of the slice: x: 2, y: 2, z: 4, core: 2. Of those that a mesh axis runs over, the one named last changes fastest.
Arguments:
- hidden_in: bfloat16 [4096, 4096], P(('groups', 'ctx'), 'head'), parts along dimension 0, may hold values from -6 to 6
- attn_gain: float32 [4096], replicated, may hold values from 0.5 to 12, as said below
- w_query: bfloat16 [4096, 2048], P(None, 'head'), may hold values from -0.09375 to 0.09375
- w_keys: bfloat16 [4096, 1024], P(None, 'head'), may hold values from -0.09375 to 0.09375
- w_values: bfloat16 [4096, 1024], P(None, 'head'), may hold values from -0.09375 to 0.09375
- wo_attn: bfloat16 [2048, 4096], P('head'), may hold values from -0.125 to 0.125
- lin_gain: float32 [4096], replicated, may hold values from 0.5 to 1.5
- w_feature: bfloat16 [4096, 256], P(None, 'head'), may hold values from -0.09375 to 0.09375
- wv_linear: bfloat16 [4096, 2048], P(None, 'head'), may hold values from -0.09375 to 0.09375
- out_gain: float32 [8, 256], P('head'), may hold values from 0.5 to 1.5
- wo_linear: bfloat16 [2048, 4096], P('head'), may hold values from -0.125 to 0.125
- entry_state: float32 [16, 273, 256], P(('groups', 'head')), parts along dimension 0, may hold values from -180 to 180
Outputs:
- mixed: bfloat16 [4096, 4096], P(('groups', 'ctx'), 'head'), parts along dimension 0
There are 2 independent parts, one for each index of `groups`. A program takes and returns all parts, laid end to end along the dimension named above; an argument that names none is the same for every part. Nothing has to cross between parts.
Inputs may be any that keep to these rules, and one draw needn't show every extreme that they name: `attn_gain`: a positive gain for every feature.
All inputs are finite; a program needn't handle non-finite values.
Results may differ from a plain program's by a relative error of at most 0.008.
The roundings to bfloat16 on the way count: a program that leaves them out, or rounds other values in their place, can miss the bound.
Values may be sent and summed in bfloat16 or wider, within the bound.
No kernel may reach another device: no remote copies, remote signals or barrier semaphores. Data moves between devices by JAX's collectives and lax.ppermute only.
A program may use at most 128 MiB of HBM per device.

v0:
```python
import math
import jax
import jax.numpy as jnp
from jax import lax
from jax.sharding import PartitionSpec as P

HEAD = 128
WINDOW = 64
FEAT = 16
VDIM = 256


def from_behind(value, axis, by):
    devices = lax.axis_size(axis)
    pairs = [(i, i + by) for i in range(devices) if 0 <= i + by < devices]
    return lax.ppermute(value, axis, pairs)


def norm_rows(values, gain):
    wide = values.astype(jnp.float32)
    scale = lax.rsqrt(jnp.mean(wide * wide, axis=-1, keepdims=True) + 1e-05)
    return (wide * scale * gain).astype(jnp.bfloat16)


def taylor(inputs):
    width = inputs.shape[-1]
    outer = (inputs[..., :, None] * inputs[..., None, :]).reshape(
        inputs.shape[:-1] + (width * width,)
    )
    ones = jnp.ones(inputs.shape[:-1] + (1,), jnp.float32)
    return jnp.concatenate(
        [ones, inputs / width**0.25, outer / (math.sqrt(2.0) * math.sqrt(width))], axis=-1
    )


def body(
    hidden_in,
    attn_gain,
    w_query,
    w_keys,
    w_values,
    wo_attn,
    lin_gain,
    w_feature,
    wv_linear,
    out_gain,
    wo_linear,
    entry_state,
):
    tok_rows = hidden_in.shape[0]
    whole = lax.all_gather(hidden_in, "head", axis=1, tiled=True)
    normed = norm_rows(whole, attn_gain)
    query = jnp.dot(normed, w_query, preferred_element_type=jnp.float32).astype(jnp.bfloat16)
    keys = jnp.dot(normed, w_keys, preferred_element_type=jnp.float32).astype(jnp.bfloat16)
    values = jnp.dot(normed, w_values, preferred_element_type=jnp.float32).astype(jnp.bfloat16)
    kv_cols = keys.shape[1]
    kv_heads = kv_cols // HEAD
    group = query.shape[1] // HEAD // kv_heads
    kv_pair = jnp.concatenate([keys, values], axis=1)
    rim = from_behind(kv_pair[tok_rows - WINDOW :], "ctx", 1)
    kv_all = jnp.concatenate([rim, kv_pair], axis=0)
    key_all = kv_all[:, :kv_cols].reshape(tok_rows + WINDOW, kv_heads, HEAD)
    value_all = kv_all[:, kv_cols:].reshape(tok_rows + WINDOW, kv_heads, HEAD)
    query_heads = query.reshape(tok_rows, kv_heads, group, HEAD)
    scores = jnp.einsum(
        "tkgd,skd->kgts", query_heads, key_all, preferred_element_type=jnp.float32
    ) / math.sqrt(HEAD)
    start = lax.axis_index("ctx") * tok_rows
    qpos = start + jnp.arange(tok_rows, dtype=jnp.int32)
    kpos = start - WINDOW + jnp.arange(tok_rows + WINDOW, dtype=jnp.int32)
    visible = (
        (kpos[None, :] <= qpos[:, None])
        & (kpos[None, :] > qpos[:, None] - WINDOW)
        & (kpos[None, :] >= 0)
    )
    scores = jnp.where(visible, scores, -jnp.inf)
    top = jnp.max(scores, axis=-1, keepdims=True)
    expd = jnp.exp(scores - top)
    probs = (expd / jnp.sum(expd, axis=-1, keepdims=True)).astype(jnp.bfloat16)
    attended = jnp.einsum("kgts,skd->tkgd", probs, value_all, preferred_element_type=jnp.float32)
    attended = attended.astype(jnp.bfloat16).reshape(tok_rows, -1)
    terms = jnp.dot(attended, wo_attn, preferred_element_type=jnp.float32)
    partial_out = lax.psum_scatter(terms, "head", scatter_dimension=1, tiled=True)
    after_window = (hidden_in.astype(jnp.float32) + partial_out).astype(jnp.bfloat16)
    after_whole = lax.all_gather(after_window, "head", axis=1, tiled=True)
    normed2 = norm_rows(after_whole, lin_gain)
    feats = jnp.dot(normed2, w_feature, preferred_element_type=jnp.float32)
    lin_heads = feats.shape[1] // (2 * FEAT)
    feats = feats.reshape(tok_rows, lin_heads, 2, FEAT)
    query_feat = feats[:, :, 0, :]
    key_feat = feats[:, :, 1, :]
    lvalues = (
        jnp.dot(normed2, wv_linear, preferred_element_type=jnp.float32)
        .astype(jnp.bfloat16)
        .reshape(tok_rows, lin_heads, VDIM)
    )
    phi_query = taylor(query_feat)
    phi_key = taylor(key_feat)
    highest = lax.Precision.HIGHEST
    local_state = jnp.einsum(
        "thf,thv->hfv", phi_key, lvalues.astype(jnp.float32), precision=highest
    )
    ctx_count = lax.axis_size("ctx")
    every = (
        lax.all_gather(local_state.astype(jnp.bfloat16), "ctx", axis=0, tiled=True)
        .astype(local_state.dtype)
        .reshape((ctx_count,) + local_state.shape)
    )
    earlier = (jnp.arange(ctx_count, dtype=jnp.int32) < lax.axis_index("ctx")).astype(jnp.float32)
    prior = jnp.einsum("c,chfv->hfv", earlier, every, precision=highest)
    carried = entry_state + prior
    cross = jnp.einsum("thf,hfv->thv", phi_query, carried, precision=highest)
    sims = jnp.einsum("thf,shf->hts", query_feat, key_feat, precision=highest) / math.sqrt(FEAT)
    causal = jnp.arange(tok_rows)[:, None] >= jnp.arange(tok_rows)[None, :]
    weights = jnp.where(causal[None], 1.0 + sims + 0.5 * sims * sims, 0.0).astype(jnp.bfloat16)
    intra = jnp.einsum("hts,shv->thv", weights, lvalues, preferred_element_type=jnp.float32)
    lin_out = cross + intra
    scale = lax.rsqrt(jnp.mean(lin_out * lin_out, axis=-1, keepdims=True) + 1e-05)
    lin_normed = (
        (lin_out * scale * out_gain[None]).astype(jnp.bfloat16).reshape(tok_rows, lin_heads * VDIM)
    )
    lin_terms = jnp.dot(lin_normed, wo_linear, preferred_element_type=jnp.float32)
    lin_part = lax.psum_scatter(lin_terms, "head", scatter_dimension=1, tiled=True)
    return (after_window.astype(jnp.float32) + lin_part).astype(jnp.bfloat16)


def solution(mesh):
    in_specs = (
        P(("groups", "ctx"), "head"),
        P(),
        P(None, "head"),
        P(None, "head"),
        P(None, "head"),
        P("head", None),
        P(),
        P(None, "head"),
        P(None, "head"),
        P("head", None),
        P("head", None),
        P(("groups", "head"), None, None),
    )
    out_specs = P(("groups", "ctx"), "head")
    return jax.shard_map(body, mesh=mesh, in_specs=in_specs, out_specs=out_specs, check_vma=False)
```

profile of v0, /device:TPU:0, one launch (start us, length us, event | category | flops | bytes accessed | tf_op | source)
XLA Modules:
  0.0 315.9 jit_solution(14720713540210426157)
XLA Ops:
  7.7 38.4 %all-gather.4.cloned.1.call-done = bf16[512,4096]{1,0:T(8,128)(2,1)} async-done(((bf16[512,1024]{1,0:T(8,128)(2,1)}), bf16[512,4096]{1,0:T(8,128)(2,1)}) %all-gather.4.cloned.1.call-update) | async-done | bytes 4194320 | tf_op jit(solution)/shard_map/all_gather | solution.py:51
  46.1 3.2 %fusion.1 = f32[512]{0:T(512)S(1)} fusion(bf16[512,4096]{1,0:T(8,128)(2,1)} %all-gather.4.cloned.1.call-done), kind=kLoop, calls=%fused_computation.5 | loop fusion | flops 6290944 | bytes 4196352 | tf_op jit(solution)/shard_map/reduce_sum | solution.py:21
  49.6 1.6 convolution_convert_fusion.3
  51.2 1.6 convolution_convert_fusion.4
  53.0 3.6 %collective-permute-start = (bf16[64,512]{0,1:T(8,128)(2,1)S(1)}, bf16[64,512]{0,1:T(8,128)(2,1)S(1)}, u32[]{:S(2)}, u32[]{:S(2)}) collective-permute-start(bf16[64,512]{0,1:T(8,128)(2,1)S(1)} %pad_maximum_fusion), channel_id=1, source_target_pairs={{0,4},{4,8},{8,12},{1,5},{5,9},{9,13},{2,6},{6,10},{10,14},{3,7},{... | collective-permute-start | bytes 196616 | tf_op jit(solution)/shard_map/ppermute | solution.py:16
  56.6 2.6 convolution_convert_fusion.1
  59.9 3.9 %fusion.43 = (f32[2,2,512]{2,1,0:T(2,128)S(1)}, f32[2,2,512,576]{2,3,1,0:T(8,128)}) fusion(pred[512,576]{0,1:T(8,128)(4,1)S(1)} %and_and_fusion, bf16[576,2,128,1]{0,2,3,1:T(8,128)(2,1)S(1)} %bitcast.82, bf16[512,2,2,128]{0,3,2,1:T(8,128)(2,1)S(1)} %bitcast.84), kind=kOutput, calls=%fused_computation.74 | convolution fusion | flops 306709056 | bytes 5840896 | tf_op jit(solution)/shard_map/sub | solution.py:78
  63.8 3.1 fusion.13
  67.4 5.7 %fusion.44 = f32[512,4096]{1,0:T(8,128)} fusion(bf16[512,512]{0,1:T(8,128)(2,1)S(1)} %bitcast.75, bf16[512,4096]{1,0:T(8,128)(2,1)S(1)} %copy-done.3), kind=kOutput, calls=%fused_computation.75 | convolution fusion | flops 2147483648 | bytes 13107200 | tf_op jit(solution)/shard_map/dot_general | solution.py:82
  73.2 72.8 %reduce-scatter.3.cloned.1.call-done = f32[512,1024]{1,0:T(8,128)} async-done(((f32[512,4096]{1,0:T(8,128)}), f32[512,1024]{1,0:T(8,128)}) %reduce-scatter.3.cloned.1.call-update) | async-done | bytes 2097168 | tf_op jit(solution)/shard_map/reduce_scatter | solution.py:83
  146.0 2.9 add_convert_fusion.1
  149.2 34.4 %all-gather.6.cloned.1.call-done = bf16[512,4096]{1,0:T(8,128)(2,1)} async-done(((bf16[512,1024]{1,0:T(8,128)(2,1)}), bf16[512,4096]{1,0:T(8,128)(2,1)}) %all-gather.6.cloned.1.call-update) | async-done | bytes 4194320 | tf_op jit(solution)/shard_map/all_gather | solution.py:85
  183.6 3.2 %fusion.4 = f32[512]{0:T(512)S(1)} fusion(bf16[512,4096]{1,0:T(8,128)(2,1)} %all-gather.6.cloned.1.call-done), kind=kLoop, calls=%fused_computation.8 | loop fusion | flops 6290944 | bytes 4196352 | tf_op jit(solution)/shard_map/reduce_sum | solution.py:21
  187.1 1.5 fusion.15
  189.3 2.6 convolution_convert_fusion
  191.9 1.5 convolution_convert_fusion.2
  193.9 2.4 select_convert_fusion
  196.3 26.8 %all-gather.8.cloned.1.call-done = bf16[8,273,256]{2,1,0:T(8,128)(2,1)} async-done(((bf16[2,273,256]{2,1,0:T(8,128)(2,1)}), bf16[8,273,256]{2,1,0:T(8,128)(2,1)}) %all-gather.8.cloned.1.call-update) | async-done | bytes 1118224 | tf_op jit(solution)/shard_map/all_gather | solution.py:105
  223.1 2.0 fusion.26
  225.1 1.5 bitcast_add_fusion
  226.7 2.0 fusion.21
  229.4 5.7 %fusion.45 = f32[512,4096]{1,0:T(8,128)} fusion(bf16[512,512]{0,1:T(8,128)(2,1)S(1)} %bitcast.73, bf16[512,4096]{1,0:T(8,128)(2,1)S(1)} %copy-done.4), kind=kOutput, calls=%fused_computation.76 | convolution fusion | flops 2147483648 | bytes 13107200 | tf_op jit(solution)/shard_map/dot_general | solution.py:122
  235.1 71.3 %reduce-scatter.5.cloned.1.call-done = f32[512,1024]{1,0:T(8,128)} async-done(((f32[512,4096]{1,0:T(8,128)}), f32[512,1024]{1,0:T(8,128)}) %reduce-scatter.5.cloned.1.call-update) | async-done | bytes 2097168 | tf_op jit(solution)/shard_map/reduce_scatter | solution.py:123
  306.5 2.9 add_convert_fusion
  (63 shorter events, 5.1 us)
Async XLA Ops:
  6.5 42.8 %copy-start = (bf16[4096,256]{1,0:T(8,128)(2,1)S(1)}, bf16[4096,256]{1,0:T(8,128)(2,1)}, u32[]{:S(2)}) copy-start(bf16[4096,256]{1,0:T(8,128)(2,1)} %param.16) | copy-start | bytes 6291460
  6.5 42.8 %copy-start.15 = (f32[4096]{0:T(1024)S(1)}, f32[4096]{0:T(1024)}, u32[]{:S(2)}) copy-start(f32[4096]{0:T(1024)} %param.13) | copy-start | bytes 49156
  6.5 39.6 %all-gather.4.cloned.1.call-start = ((), (), s32[]{:S(2)}) async-start(), calls=%async_computation.2 | async-start | bytes 5242880 | tf_op jit(solution)/shard_map/all_gather | solution.py:51
  7.3 138.8 %reduce-scatter.3.cloned.1.call-start = ((), (), s32[]{:S(2)}) async-start(), calls=%async_computation.3 | async-start | bytes 10485760 | tf_op jit(solution)/shard_map/reduce_scatter | solution.py:83
  46.1 3.4 %copy-start.5 = (bf16[512,4096]{1,0:T(8,128)(2,1)S(1)}, bf16[512,4096]{1,0:T(8,128)(2,1)}, u32[]{:S(2)}) copy-start(bf16[512,4096]{1,0:T(8,128)(2,1)} %all-gather.4.cloned.1.call-done) | copy-start | bytes 12582916
  49.6 1.6 copy-start.13
  51.2 5.3 %copy-start.11 = (bf16[4096,512]{1,0:T(8,128)(2,1)S(1)}, bf16[4096,512]{1,0:T(8,128)(2,1)}, u32[]{:S(2)}) copy-start(bf16[4096,512]{1,0:T(8,128)(2,1)} %param.14) | copy-start | bytes 12582916
  53.0 6.5 %collective-permute-start = (bf16[64,512]{0,1:T(8,128)(2,1)S(1)}, bf16[64,512]{0,1:T(8,128)(2,1)S(1)}, u32[]{:S(2)}, u32[]{:S(2)}) collective-permute-start(bf16[64,512]{0,1:T(8,128)(2,1)S(1)} %pad_maximum_fusion), channel_id=1, source_target_pairs={{0,4},{4,8},{8,12},{1,5},{5,9},{9,13},{2,6},{6,10},{10,14},{3,7},{... | collective-permute-start | bytes 196616 | tf_op jit(solution)/shard_map/ppermute | solution.py:16
  63.8 3.6 %copy-start.3 = (bf16[512,4096]{1,0:T(8,128)(2,1)S(1)}, bf16[512,4096]{1,0:T(8,128)(2,1)}, u32[]{:S(2)}) copy-start(bf16[512,4096]{1,0:T(8,128)(2,1)} %param.17) | copy-start | bytes 12582916
  73.1 72.9 %copy-start.7 = (bf16[512,1024]{1,0:T(8,128)(2,1)S(1)}, bf16[512,1024]{1,0:T(8,128)(2,1)}, u32[]{:S(2)}) copy-start(bf16[512,1024]{1,0:T(8,128)(2,1)} %param.12) | copy-start | bytes 3145732
  73.2 113.7 %copy-start.14 = (bf16[4096,64]{0,1:T(8,128)(2,1)S(1)}, bf16[4096,64]{0,1:T(8,128)(2,1)}, u32[]{:S(2)}) copy-start(bf16[4096,64]{0,1:T(8,128)(2,1)} %param.19) | copy-start | bytes 1572868
  73.2 113.7 %copy-start.16 = (f32[4096]{0:T(1024)S(1)}, f32[4096]{0:T(1024)}, u32[]{:S(2)}) copy-start(f32[4096]{0:T(1024)} %param.18) | copy-start | bytes 49156
  73.2 110.4 %all-gather.6.cloned.1.call-start = ((), (), s32[]{:S(2)}) async-start(), calls=%async_computation.4 | async-start | bytes 5242880 | tf_op jit(solution)/shard_map/all_gather | solution.py:85
  149.0 74.2 %all-gather.8.cloned.1.call-start = ((), (), s32[]{:S(2)}) async-start(), calls=%async_computation.5 | async-start | bytes 1433600 | tf_op jit(solution)/shard_map/all_gather | solution.py:105
  183.6 3.4 %copy-start.6 = (bf16[512,4096]{1,0:T(8,128)(2,1)S(1)}, bf16[512,4096]{1,0:T(8,128)(2,1)}, u32[]{:S(2)}) copy-start(bf16[512,4096]{1,0:T(8,128)(2,1)} %all-gather.6.cloned.1.call-done) | copy-start | bytes 12582916
  187.1 2.2 copy-start.12
  191.9 31.3 %copy-start.8 = (bf16[512,512]{0,1:T(8,128)(2,1)}, bf16[512,512]{0,1:T(8,128)(2,1)S(1)}, u32[]{:S(2)}) copy-start(bf16[512,512]{0,1:T(8,128)(2,1)S(1)} %convolution_convert_fusion) | copy-start | bytes 1572868
  193.4 113.0 %reduce-scatter.5.cloned.1.call-start = ((), (), s32[]{:S(2)}) async-start(), calls=%async_computation.6 | async-start | bytes 10485760 | tf_op jit(solution)/shard_map/reduce_scatter | solution.py:123
  225.1 3.6 %copy-start.9 = (bf16[512,512]{0,1:T(8,128)(2,1)S(1)}, bf16[512,512]{0,1:T(8,128)(2,1)}, u32[]{:S(2)}) copy-start(bf16[512,512]{0,1:T(8,128)(2,1)} %copy-done.8) | copy-start | bytes 1572868
  225.1 4.1 %copy-start.10 = (f32[2,256]{1,0:T(2,128)S(1)}, f32[2,256]{1,0:T(2,128)}, u32[]{:S(2)}) copy-start(f32[2,256]{1,0:T(2,128)} %param.21) | copy-start | bytes 6148
  226.6 2.7 copy-start.4
  235.1 71.4 %copy-start.2 = (bf16[512,1024]{1,0:T(8,128)(2,1)S(1)}, bf16[512,1024]{1,0:T(8,128)(2,1)}, u32[]{:S(2)}) copy-start(bf16[512,1024]{1,0:T(8,128)(2,1)} %add_convert_fusion.1) | copy-start | bytes 3145732
  235.1 74.3 %copy-start.1 = (bf16[4096,256]{1,0:T(8,128)(2,1)S(1)}, bf16[4096,256]{1,0:T(8,128)(2,1)}, u32[]{:S(2)}) copy-start(bf16[4096,256]{1,0:T(8,128)(2,1)} %param.16) | copy-start | bytes 6291460
Sparse Core Ops, SparseCore 0:
  8.9 37.1 all-gather.3
  73.3 72.6 reduce-scatter.2
  149.1 34.4 all-gather.5
  193.5 29.5 all-gather.7
  235.2 71.1 reduce-scatter.4
where the time goes:
time: 316 us
  waiting for transfers between devices  245 us (78%)
  matrix products  36.6 us (12%)
  other arithmetic  15.1 us (5%)
  between operations  13.5 us (4%)
  starting transfers between devices  4.22 us (1%)
    reduce_scatter x1, waiting for transfers between devices, body(): lax.psum_scatter(terms, 'head', scatter_dimension=1, tiled=True)  72.8 us
    reduce_scatter x1, waiting for transfers between devices, body(): lax.psum_scatter(lin_terms, 'head', scatter_dimension=1, tiled=True)  71.3 us
    all_gather x1, waiting for transfers between devices, body(): whole = lax.all_gather(hidden_in, 'head', axis=1, tiled=True)  38.4 us
    all_gather x1, waiting for transfers between devices, body(): after_whole = lax.all_gather(after_window, 'head', axis=1, tiled=True)  34.4 us
    all_gather x1, waiting for transfers between devices, body(): lax.all_gather(local_state.astype(jnp.bfloat16), 'ctx', axis=0, tiled=True)  26.8 us
    reduce_sum x2, other arithmetic, norm_rows(): scale = lax.rsqrt(jnp.mean(wide * wide, axis=-1, keepdims=True) + 1e-05)  6.46 us
  transfers between devices with their start and end apart: 6, of which 6 were waited for; matrix products, arithmetic and copies ran while one was open for 2% of the time, Pallas kernels for 0%

commit v1 on v0

--- a/solution.py
+++ b/solution.py
@@ -8,6 +8,24 @@
 WINDOW = 64
 FEAT = 16
 VDIM = 256
+
+
+def set_grid(vec):
+    before, work_now, extra = (lax.axis_size("ctx"), lax.axis_index("ctx"), vec.shape[0])
+    sheets = tuple((i0 * before if b == 0 else i0 for b, i0 in enumerate(vec.shape)))
+    z = then = vec
+    tmp = lax.dynamic_update_slice_in_dim(
+        jnp.zeros(sheets, vec.dtype), vec, work_now * extra, axis=0
+    )
+    for no in range(1, before // 2 + 1):
+        z = lax.ppermute(z, "ctx", tuple(((b, (b + 1) % before) for b in range(before))))
+        tmp = lax.dynamic_update_slice_in_dim(tmp, z, (work_now - no) % before * extra, axis=0)
+        if 2 * no < before:
+            then = lax.ppermute(then, "ctx", tuple(((b, (b - 1) % before) for b in range(before))))
+            tmp = lax.dynamic_update_slice_in_dim(
+                tmp, then, (work_now + no) % before * extra, axis=0
+            )
+    return tmp
 
 
 def from_behind(value, axis, by):
@@ -102,7 +120,7 @@
     )
     ctx_count = lax.axis_size("ctx")
     every = (
-        lax.all_gather(local_state.astype(jnp.bfloat16), "ctx", axis=0, tiled=True)
+        set_grid(local_state.astype(jnp.bfloat16))
         .astype(local_state.dtype)
         .reshape((ctx_count,) + local_state.shape)
     )

time: 316 us -> 306 us (0.968)
  waiting for transfers between devices: 245 us -> 233 us
  starting transfers between devices: 4.22 us -> 7.8 us
    all_gather x1 -> x0, waiting for transfers between devices: 26.8 us -> none  [body(): lax.all_gather(local_state.astype(jnp.bfloat16), 'ctx', axis=0, tiled=True)]
    ppermute x0 -> x3, waiting for transfers between devices: none -> 16.5 us  [the longest x2 11.4 us: set_grid(): lax.ppermute(z, 'ctx', tuple(((b, (b + 1) % before) for b in range(before...]
    ppermute x0 -> x3, starting transfers between devices: none -> 3.88 us  [the longest x1 2.39 us: set_grid(): lax.ppermute(then, 'ctx', tuple(((b, (b - 1) % before) for b in range(bef...]
  transfers between devices with their start and end apart: 6 -> 8, of which waited for: 6 -> 8; matrix products, arithmetic and copies ran while one was open for 2% -> 2% of each run, Pallas kernels for 0% -> 0%
where the time goes in v1:
time: 306 us
  waiting for transfers between devices  233 us (76%)
  matrix products  34.7 us (11%)
  other arithmetic  14 us (5%)
  between operations  13.6 us (4%)
  starting transfers between devices  7.8 us (3%)
    reduce_scatter x1, waiting for transfers between devices, body(): lax.psum_scatter(terms, 'head', scatter_dimension=1, tiled=True)  72.8 us
    reduce_scatter x1, waiting for transfers between devices, body(): lax.psum_scatter(lin_terms, 'head', scatter_dimension=1, tiled=True)  70 us
    all_gather x1, waiting for transfers between devices, body(): whole = lax.all_gather(hidden_in, 'head', axis=1, tiled=True)  38.4 us
    all_gather x1, waiting for transfers between devices, body(): after_whole = lax.all_gather(after_window, 'head', axis=1, tiled=True)  34.4 us
    ppermute x2, waiting for transfers between devices, set_grid(): lax.ppermute(z, 'ctx', tuple(((b, (b + 1) % before) for b in range(before...  11.4 us
    reduce_sum x2, other arithmetic, norm_rows(): scale = lax.rsqrt(jnp.mean(wide * wide, axis=-1, keepdims=True) + 1e-05)  6.46 us
  transfers between devices with their start and end apart: 8, of which 8 were waited for; matrix products, arithmetic and copies ran while one was open for 2% of the time, Pallas kernels for 0%

profile of v1, /device:TPU:0, one launch (start us, length us, event | category | flops | bytes accessed | tf_op | source)
XLA Modules:
  0.0 306.0 jit_solution(17949677367431826794)
XLA Ops:
  7.7 38.4 %all-gather.3.cloned.1.call-done = bf16[512,4096]{1,0:T(8,128)(2,1)} async-done(((bf16[512,1024]{1,0:T(8,128)(2,1)}), bf16[512,4096]{1,0:T(8,128)(2,1)}) %all-gather.3.cloned.1.call-update) | async-done | bytes 4194320 | tf_op jit(solution)/shard_map/all_gather | solution.py:69
  46.1 3.2 %fusion.1 = f32[512]{0:T(512)S(1)} fusion(bf16[512,4096]{1,0:T(8,128)(2,1)} %all-gather.3.cloned.1.call-done), kind=kLoop, calls=%fused_computation.5 | loop fusion | flops 6290944 | bytes 4196352 | tf_op jit(solution)/shard_map/reduce_sum | solution.py:39
  49.6 1.6 convolution_convert_fusion.4
  51.2 1.6 convolution_convert_fusion.3
  53.0 3.6 %collective-permute-start = (bf16[64,512]{0,1:T(8,128)(2,1)S(1)}, bf16[64,512]{0,1:T(8,128)(2,1)S(1)}, u32[]{:S(2)}, u32[]{:S(2)}) collective-permute-start(bf16[64,512]{0,1:T(8,128)(2,1)S(1)} %pad_maximum_fusion), channel_id=1, source_target_pairs={{0,4},{4,8},{8,12},{1,5},{5,9},{9,13},{2,6},{6,10},{10,14},{3,7},{... | collective-permute-start | bytes 196616 | tf_op jit(solution)/shard_map/ppermute | solution.py:34
  56.6 2.6 convolution_convert_fusion.1
  59.9 3.9 %fusion.43 = (f32[2,2,512]{2,1,0:T(2,128)S(1)}, f32[2,2,512,576]{2,3,1,0:T(8,128)}) fusion(pred[512,576]{0,1:T(8,128)(4,1)S(1)} %and_and_fusion, bf16[576,2,128,1]{0,2,3,1:T(8,128)(2,1)S(1)} %bitcast.83, bf16[512,2,2,128]{0,3,2,1:T(8,128)(2,1)S(1)} %bitcast.84), kind=kOutput, calls=%fused_computation.78 | convolution fusion | flops 306709056 | bytes 5840896 | tf_op jit(solution)/shard_map/sub | solution.py:96
  63.8 3.1 %fusion.13 = bf16[2,128,2,512]{3,1,2,0:T(8,128)(2,1)S(1)} fusion(bf16[576,2,128,1]{0,2,3,1:T(8,128)(2,1)S(1)} %bitcast.82, f32[2,2,512,576]{2,3,1,0:T(8,128)} %get-tuple-element.12, f32[2,2,512]{2,1,0:T(2,128)S(1)} %get-tuple-element.11), kind=kOutput, calls=%fused_computation.26 | convolution fusion | flops 304611328 | bytes 5545984 | tf_op jit(solution)/shard_map/kgts,skd->tkgd/dot_general | solution.py:98
  67.4 5.7 %fusion.44 = f32[512,4096]{1,0:T(8,128)} fusion(bf16[512,512]{0,1:T(8,128)(2,1)S(1)} %bitcast.78, bf16[512,4096]{1,0:T(8,128)(2,1)S(1)} %copy-done.3), kind=kOutput, calls=%fused_computation.79 | convolution fusion | flops 2147483648 | bytes 13107200 | tf_op jit(solution)/shard_map/dot_general | solution.py:100
  73.2 72.8 %reduce-scatter.3.cloned.1.call-done = f32[512,1024]{1,0:T(8,128)} async-done(((f32[512,4096]{1,0:T(8,128)}), f32[512,1024]{1,0:T(8,128)}) %reduce-scatter.3.cloned.1.call-update) | async-done | bytes 2097168 | tf_op jit(solution)/shard_map/reduce_scatter | solution.py:101
  146.0 2.9 add_convert_fusion.1
  149.3 34.4 %all-gather.5.cloned.1.call-done = bf16[512,4096]{1,0:T(8,128)(2,1)} async-done(((bf16[512,1024]{1,0:T(8,128)(2,1)}), bf16[512,4096]{1,0:T(8,128)(2,1)}) %all-gather.5.cloned.1.call-update) | async-done | bytes 4194320 | tf_op jit(solution)/shard_map/all_gather | solution.py:103
  183.6 3.2 %fusion.4 = f32[512]{0:T(512)S(1)} fusion(bf16[512,4096]{1,0:T(8,128)(2,1)} %all-gather.5.cloned.1.call-done), kind=kLoop, calls=%fused_computation.8 | loop fusion | flops 6290944 | bytes 4196352 | tf_op jit(solution)/shard_map/reduce_sum | solution.py:39
  189.2 2.6 convolution_convert_fusion
  193.8 1.5 collective-permute-start.1
  195.4 2.4 collective-permute-start.2
  197.8 2.3 select_convert_fusion
  200.2 5.1 %collective-permute-done.1 = bf16[2,273,256]{2,1,0:T(8,128)(2,1)S(1)} collective-permute-done((bf16[2,273,256]{2,1,0:T(8,128)(2,1)S(1)}, bf16[2,273,256]{2,1,0:T(8,128)(2,1)S(1)}, u32[]{:S(2)}, u32[]{:S(2)}) %collective-permute-start.1) | collective-permute-done | bytes 279584 | tf_op jit(solution)/shard_map/ppermute | solution.py:21
  205.5 5.1 %collective-permute-done.2 = bf16[2,273,256]{2,1,0:T(8,128)(2,1)S(1)} collective-permute-done((bf16[2,273,256]{2,1,0:T(8,128)(2,1)S(1)}, bf16[2,273,256]{2,1,0:T(8,128)(2,1)S(1)}, u32[]{:S(2)}, u32[]{:S(2)}) %collective-permute-start.2) | collective-permute-done | bytes 279584 | tf_op jit(solution)/shard_map/ppermute | solution.py:24
  210.6 6.3 %collective-permute-done.3 = bf16[2,273,256]{2,1,0:T(8,128)(2,1)S(1)} collective-permute-done((bf16[2,273,256]{2,1,0:T(8,128)(2,1)S(1)}, bf16[2,273,256]{2,1,0:T(8,128)(2,1)S(1)}, u32[]{:S(2)}, u32[]{:S(2)}) %collective-permute-start.3) | collective-permute-done | bytes 279584 | tf_op jit(solution)/shard_map/ppermute | solution.py:21
  218.1 2.0 fusion.21
  220.8 5.7 %fusion.45 = f32[512,4096]{1,0:T(8,128)} fusion(bf16[512,512]{0,1:T(8,128)(2,1)S(1)} %bitcast.74, bf16[512,4096]{1,0:T(8,128)(2,1)S(1)} %copy-done.4), kind=kOutput, calls=%fused_computation.80 | convolution fusion | flops 2147483648 | bytes 13107200 | tf_op jit(solution)/shard_map/dot_general | solution.py:140
  226.5 70.0 %reduce-scatter.5.cloned.1.call-done = f32[512,1024]{1,0:T(8,128)} async-done(((f32[512,4096]{1,0:T(8,128)}), f32[512,1024]{1,0:T(8,128)}) %reduce-scatter.5.cloned.1.call-update) | async-done | bytes 2097168 | tf_op jit(solution)/shard_map/reduce_scatter | solution.py:141
  296.6 2.9 add_convert_fusion
  (72 shorter events, 9.4 us)
Async XLA Ops:
  6.5 42.8 %copy-start = (bf16[4096,256]{1,0:T(8,128)(2,1)S(1)}, bf16[4096,256]{1,0:T(8,128)(2,1)}, u32[]{:S(2)}) copy-start(bf16[4096,256]{1,0:T(8,128)(2,1)} %param.15) | copy-start | bytes 6291460
  6.5 42.8 %copy-start.16 = (f32[4096]{0:T(1024)S(1)}, f32[4096]{0:T(1024)}, u32[]{:S(2)}) copy-start(f32[4096]{0:T(1024)} %param.13) | copy-start | bytes 49156
  6.5 39.6 %all-gather.3.cloned.1.call-start = ((), (), s32[]{:S(2)}) async-start(), calls=%async_computation.2 | async-start | bytes 5242880 | tf_op jit(solution)/shard_map/all_gather | solution.py:69
  7.3 138.8 %reduce-scatter.3.cloned.1.call-start = ((), (), s32[]{:S(2)}) async-start(), calls=%async_computation.3 | async-start | bytes 10485760 | tf_op jit(solution)/shard_map/reduce_scatter | solution.py:101
  46.1 3.4 %copy-start.5 = (bf16[512,4096]{1,0:T(8,128)(2,1)S(1)}, bf16[512,4096]{1,0:T(8,128)(2,1)}, u32[]{:S(2)}) copy-start(bf16[512,4096]{1,0:T(8,128)(2,1)} %all-gather.3.cloned.1.call-done) | copy-start | bytes 12582916
  51.2 5.3 %copy-start.12 = (bf16[4096,512]{1,0:T(8,128)(2,1)S(1)}, bf16[4096,512]{1,0:T(8,128)(2,1)}, u32[]{:S(2)}) copy-start(bf16[4096,512]{1,0:T(8,128)(2,1)} %param.14) | copy-start | bytes 12582916
  53.0 6.5 %collective-permute-start = (bf16[64,512]{0,1:T(8,128)(2,1)S(1)}, bf16[64,512]{0,1:T(8,128)(2,1)S(1)}, u32[]{:S(2)}, u32[]{:S(2)}) collective-permute-start(bf16[64,512]{0,1:T(8,128)(2,1)S(1)} %pad_maximum_fusion), channel_id=1, source_target_pairs={{0,4},{4,8},{8,12},{1,5},{5,9},{9,13},{2,6},{6,10},{10,14},{3,7},{... | collective-permute-start | bytes 196616 | tf_op jit(solution)/shard_map/ppermute | solution.py:34
  63.8 3.6 %copy-start.3 = (bf16[512,4096]{1,0:T(8,128)(2,1)S(1)}, bf16[512,4096]{1,0:T(8,128)(2,1)}, u32[]{:S(2)}) copy-start(bf16[512,4096]{1,0:T(8,128)(2,1)} %param.17) | copy-start | bytes 12582916
  73.1 72.9 %copy-start.7 = (bf16[512,1024]{1,0:T(8,128)(2,1)S(1)}, bf16[512,1024]{1,0:T(8,128)(2,1)}, u32[]{:S(2)}) copy-start(bf16[512,1024]{1,0:T(8,128)(2,1)} %param.12) | copy-start | bytes 3145732
  73.2 113.7 %copy-start.15 = (bf16[4096,64]{0,1:T(8,128)(2,1)S(1)}, bf16[4096,64]{0,1:T(8,128)(2,1)}, u32[]{:S(2)}) copy-start(bf16[4096,64]{0,1:T(8,128)(2,1)} %param.19) | copy-start | bytes 1572868
  73.2 113.7 %copy-start.17 = (f32[4096]{0:T(1024)S(1)}, f32[4096]{0:T(1024)}, u32[]{:S(2)}) copy-start(f32[4096]{0:T(1024)} %param.18) | copy-start | bytes 49156
  73.2 110.4 %all-gather.5.cloned.1.call-start = ((), (), s32[]{:S(2)}) async-start(), calls=%async_computation.4 | async-start | bytes 5242880 | tf_op jit(solution)/shard_map/all_gather | solution.py:103
  149.0 147.6 %reduce-scatter.5.cloned.1.call-start = ((), (), s32[]{:S(2)}) async-start(), calls=%async_computation.5 | async-start | bytes 10485760 | tf_op jit(solution)/shard_map/reduce_scatter | solution.py:141
  183.6 3.4 %copy-start.6 = (bf16[512,4096]{1,0:T(8,128)(2,1)S(1)}, bf16[512,4096]{1,0:T(8,128)(2,1)}, u32[]{:S(2)}) copy-start(bf16[512,4096]{1,0:T(8,128)(2,1)} %all-gather.5.cloned.1.call-done) | copy-start | bytes 12582916
  187.1 2.2 copy-start.13
  193.8 11.5 %collective-permute-start.1 = (bf16[2,273,256]{2,1,0:T(8,128)(2,1)S(1)}, bf16[2,273,256]{2,1,0:T(8,128)(2,1)S(1)}, u32[]{:S(2)}, u32[]{:S(2)}) collective-permute-start(bf16[2,273,256]{2,1,0:T(8,128)(2,1)S(1)} %get-tuple-element.14), channel_id=1, source_target_pairs={{0,4},{4,8},{8,12},{12,0},{1,5},{5,9},{9,13},{13,1},{2,6},{6,10},{... | collective-permute-start | bytes 838664 | tf_op jit(solution)/shard_map/ppermute | solution.py:21
  195.4 10.0 %copy-start.9 = (bf16[8,273,256]{2,1,0:T(8,128)(2,1)S(1)}, bf16[8,273,256]{2,1,0:T(8,128)(2,1)}, u32[]{:S(2)}) copy-start(bf16[8,273,256]{2,1,0:T(8,128)(2,1)} %copy-done.8) | copy-start | bytes 3354628
  195.4 22.2 %copy-start.10 = (f32[2,273,256]{2,0,1:T(2,128)S(1)}, f32[2,273,256]{2,0,1:T(2,128)}, u32[]{:S(2)}) copy-start(f32[2,273,256]{2,0,1:T(2,128)} %param.23) | copy-start | bytes 1677316
  195.4 15.2 %collective-permute-start.2 = (bf16[2,273,256]{2,1,0:T(8,128)(2,1)S(1)}, bf16[2,273,256]{2,1,0:T(8,128)(2,1)S(1)}, u32[]{:S(2)}, u32[]{:S(2)}) collective-permute-start(bf16[2,273,256]{2,1,0:T(8,128)(2,1)S(1)} %get-tuple-element.14), channel_id=1, source_target_pairs={{0,12},{4,0},{8,4},{12,8},{1,13},{5,1},{9,5},{13,9},{2,14},{6,2},{... | collective-permute-start | bytes 838664 | tf_op jit(solution)/shard_map/ppermute | solution.py:24
  205.3 11.6 %collective-permute-start.3 = (bf16[2,273,256]{2,1,0:T(8,128)(2,1)S(1)}, bf16[2,273,256]{2,1,0:T(8,128)(2,1)S(1)}, u32[]{:S(2)}, u32[]{:S(2)}) collective-permute-start(bf16[2,273,256]{2,1,0:T(8,128)(2,1)S(1)} %collective-permute-done.1), channel_id=1, source_target_pairs={{0,4},{4,8},{8,12},{12,0},{1,5},{5,9},{9,13},{13,1},{2,6},{6,10},{... | collective-permute-start | bytes 838664 | tf_op jit(solution)/shard_map/ppermute | solution.py:21
  217.7 3.0 copy-start.11
  218.1 2.7 copy-start.4
  226.5 70.0 %copy-start.2 = (bf16[512,1024]{1,0:T(8,128)(2,1)S(1)}, bf16[512,1024]{1,0:T(8,128)(2,1)}, u32[]{:S(2)}) copy-start(bf16[512,1024]{1,0:T(8,128)(2,1)} %add_convert_fusion.1) | copy-start | bytes 3145732
  226.5 72.9 %copy-start.1 = (bf16[4096,256]{1,0:T(8,128)(2,1)S(1)}, bf16[4096,256]{1,0:T(8,128)(2,1)}, u32[]{:S(2)}) copy-start(bf16[4096,256]{1,0:T(8,128)(2,1)} %param.15) | copy-start | bytes 6291460
  (2 other events, 2.7 us)
Sparse Core Ops, SparseCore 0:
  8.9 37.1 all-gather.2
  73.3 72.7 reduce-scatter.2
  149.1 34.4 all-gather.4
  226.7 69.8 reduce-scatter.4
